TPU v7x, 512 devices: a whole 4x8x8 slice. The times are simulated.
512 devices in a mesh: seg: 32 (over y, x), sec: 16 (over z, core).
Axes of the slice: x: 4, y: 8, z: 8, core: 2. Of those that a mesh axis runs over, the one named last changes fastest.
Arguments:
- blocks: bfloat16 [32, 4, 16, 128, 128], P('seg', None, 'sec'), may hold values from -0.5 to 0.5
- left_edge: bfloat16 [16, 128], P('sec'), may hold values from -0.5 to 0.5
- right_edge: bfloat16 [16, 128], P('sec'), may hold values from -6 to 6
- occupation: int32 [1024, 32], P(None, 'seg'), may hold values from 0 to 3
- start_sector: int32 [1024], replicated, may hold values from 0 to 15
Outputs:
- amplitude: float32 [1024], replicated
All inputs are finite; a program needn't handle non-finite values.
Results may differ from a plain program's by a relative error of at most 0.015.
Values may be sent and summed in bfloat16 or wider, within the bound.
No kernel may reach another device: no remote copies, remote signals or barrier semaphores. Data moves between devices by JAX's collectives and lax.ppermute only.
A program may use at most 64 MiB of HBM per device.

v0:
```python
import jax
import jax.numpy as jnp
from jax import lax
from jax.sharding import PartitionSpec as P


def per_device(blocks, left_edge, right_edge, occupation, start_sector):
    seg_count = lax.axis_size("seg")
    sec_count = lax.axis_size("sec")
    half_count = seg_count // 2
    seg_index = lax.axis_index("seg")
    sec_index = lax.axis_index("sec")
    is_left = seg_index < half_count
    depth = jnp.where(is_left, seg_index, seg_count - 1 - seg_index)
    conf_count = occupation.shape[0]
    sites = seg_count * occupation.shape[1]
    group = conf_count // sec_count
    width = blocks.shape[-1]
    local_states = blocks.shape[1]
    site_blocks = lax.all_gather(blocks[0], "sec", axis=1, tiled=True)
    nsec = site_blocks.shape[1]
    lefts = lax.all_gather(left_edge, "sec", axis=0, tiled=True)
    rights = lax.all_gather(right_edge, "sec", axis=0, tiled=True)
    row0 = sec_index * group
    occ_mine = lax.dynamic_slice_in_dim(occupation, row0, group, axis=0)
    occ_group = lax.all_gather(occ_mine, "seg", axis=1, tiled=True)
    start_group = lax.dynamic_slice_in_dim(start_sector, row0, group, axis=0)
    charge = jnp.array([0, 1, -1, 0], dtype=jnp.int32)
    steps = charge[occ_group]
    site_ids = jnp.arange(sites, dtype=jnp.int32)
    before = jnp.sum(jnp.where(site_ids[None, :] < seg_index, steps, 0), axis=1)
    total = jnp.sum(steps, axis=1)
    sector_here = jnp.mod(start_group + before, nsec)
    sector_end = jnp.mod(start_group + total, nsec)
    occ_here = occ_mine[:, 0]
    sector_hot = (sector_here[:, None] == jnp.arange(nsec, dtype=jnp.int32)[None, :]).astype(
        jnp.bfloat16
    )
    state_hot = (occ_here[:, None] == jnp.arange(local_states, dtype=jnp.int32)[None, :]).astype(
        jnp.float32
    )
    oriented = lax.cond(is_left, lambda b: b, lambda b: jnp.swapaxes(b, 2, 3), site_blocks)

    def apply(vector):
        spread = vector[:, None, :] * sector_hot[:, :, None]
        products = jnp.einsum("kqa,nqab->knb", spread, oriented, preferred_element_type=jnp.float32)
        return jnp.sum(products * state_hot[:, :, None], axis=1).astype(jnp.bfloat16)

    first_left = jnp.take(lefts, start_group, axis=0)
    first_right = jnp.take(rights, sector_end, axis=0)
    first = jnp.where(is_left, first_left, first_right)
    vector = jnp.where(depth == 0, first, jnp.zeros_like(first))
    chain = [(j, j + 1) for j in range(half_count - 1)] + [
        (j, j - 1) for j in range(half_count + 1, seg_count)
    ]
    for step in range(half_count):
        vector = apply(vector)
        if step < half_count - 1:
            vector = lax.ppermute(vector, "seg", chain)
    meet = [(half_count - 1, half_count), (half_count, half_count - 1)]
    other = lax.ppermute(vector, "seg", meet)
    amp = jnp.sum(vector.astype(jnp.float32) * other.astype(jnp.float32), axis=1)
    amp = jnp.where(seg_index == half_count - 1, amp, jnp.zeros_like(amp))
    gathered = lax.all_gather(amp, "sec", axis=0, tiled=True)
    return lax.psum(gathered, "seg")


def solution(mesh):
    in_specs = (
        P("seg", None, "sec", None, None),
        P("sec", None),
        P("sec", None),
        P(None, "seg"),
        P(),
    )
    out_specs = P()
    return jax.shard_map(
        per_device, mesh=mesh, in_specs=in_specs, out_specs=out_specs, check_vma=False
    )
```

profile of v0, /device:TPU:32, one launch (start us, length us, event | category | flops | bytes accessed | tf_op | source)
XLA Modules:
  0.0 317.6 jit_solution(7298248449602463857)
XLA Ops:
  6.5 1.7 copy.33
  8.2 23.3 %all-gather.2 = bf16[16,1,128]{2,1,0:T(2,128)(2,1)S(1)} all-gather(bf16[1,1,128]{2,1,0:T(2,128)(2,1)} %bitcast.200), channel_id=1, replica_groups=mesh['seg'=32,'sec'=16] {'sec'}, dimensions={0}, use_global_device_ids=true | all-gather | bytes 4352 | tf_op jit(solution)/shard_map/all_gather | solution.py:23
  31.6 14.6 %all-gather.1 = bf16[16,1,128]{2,1,0:T(2,128)(2,1)S(1)} all-gather(bf16[1,1,128]{2,1,0:T(2,128)(2,1)} %bitcast.201), channel_id=1, replica_groups=mesh['seg'=32,'sec'=16] {'sec'}, dimensions={0}, use_global_device_ids=true | all-gather | bytes 4352 | tf_op jit(solution)/shard_map/all_gather | solution.py:22
  46.9 34.2 %all-gather.3 = s32[32,1,64]{2,1,0:T(1,128)S(1)} all-gather(s32[1,1,64]{2,1,0:T(1,128)S(1)} %get-tuple-element.18), channel_id=1, replica_groups=mesh['seg'=32,'sec'=16] {'seg'}, dimensions={0}, use_global_device_ids=true | all-gather | bytes 8448 | tf_op jit(solution)/shard_map/all_gather | solution.py:26
  81.2 0.8 compare_and_fusion.1
  83.3 0.8 and_select_fusion
  84.2 3.1 conditional.1
  84.2 3.1 copy.34
  87.3 0.8 fusion.31
  88.0 1.3 collective-permute-start
  89.3 4.3 %collective-permute-done = bf16[64,128]{1,0:T(8,128)(2,1)S(1)} collective-permute-done((bf16[64,128]{1,0:T(8,128)(2,1)S(1)}, bf16[64,128]{1,0:T(8,128)(2,1)S(1)}, u32[]{:S(2)}, u32[]{:S(2)}) %collective-permute-start) | collective-permute-done | bytes 16416 | tf_op jit(solution)/shard_map/ppermute | solution.py:59
  94.4 1.3 collective-permute-start.1
  95.7 4.3 %collective-permute-done.1 = bf16[64,128]{1,0:T(8,128)(2,1)S(1)} collective-permute-done((bf16[64,128]{1,0:T(8,128)(2,1)S(1)}, bf16[64,128]{1,0:T(8,128)(2,1)S(1)}, u32[]{:S(2)}, u32[]{:S(2)}) %collective-permute-start.1) | collective-permute-done | bytes 16416 | tf_op jit(solution)/shard_map/ppermute | solution.py:59
  100.8 1.3 collective-permute-start.2
  102.1 4.3 %collective-permute-done.2 = bf16[64,128]{1,0:T(8,128)(2,1)S(1)} collective-permute-done((bf16[64,128]{1,0:T(8,128)(2,1)S(1)}, bf16[64,128]{1,0:T(8,128)(2,1)S(1)}, u32[]{:S(2)}, u32[]{:S(2)}) %collective-permute-start.2) | collective-permute-done | bytes 16416 | tf_op jit(solution)/shard_map/ppermute | solution.py:59
  107.2 1.3 collective-permute-start.3
  108.5 4.3 %collective-permute-done.3 = bf16[64,128]{1,0:T(8,128)(2,1)S(1)} collective-permute-done((bf16[64,128]{1,0:T(8,128)(2,1)S(1)}, bf16[64,128]{1,0:T(8,128)(2,1)S(1)}, u32[]{:S(2)}, u32[]{:S(2)}) %collective-permute-start.3) | collective-permute-done | bytes 16416 | tf_op jit(solution)/shard_map/ppermute | solution.py:59
  113.6 1.3 collective-permute-start.4
  114.9 4.8 %collective-permute-done.4 = bf16[64,128]{1,0:T(8,128)(2,1)S(1)} collective-permute-done((bf16[64,128]{1,0:T(8,128)(2,1)S(1)}, bf16[64,128]{1,0:T(8,128)(2,1)S(1)}, u32[]{:S(2)}, u32[]{:S(2)}) %collective-permute-start.4) | collective-permute-done | bytes 16416 | tf_op jit(solution)/shard_map/ppermute | solution.py:59
  120.4 1.3 collective-permute-start.5
  121.7 6.4 %collective-permute-done.5 = bf16[64,128]{1,0:T(8,128)(2,1)S(1)} collective-permute-done((bf16[64,128]{1,0:T(8,128)(2,1)S(1)}, bf16[64,128]{1,0:T(8,128)(2,1)S(1)}, u32[]{:S(2)}, u32[]{:S(2)}) %collective-permute-start.5) | collective-permute-done | bytes 16416 | tf_op jit(solution)/shard_map/ppermute | solution.py:59
  128.2 0.8 fusion.25
  128.9 1.3 collective-permute-start.6
  130.2 6.4 %collective-permute-done.6 = bf16[64,128]{1,0:T(8,128)(2,1)S(1)} collective-permute-done((bf16[64,128]{1,0:T(8,128)(2,1)S(1)}, bf16[64,128]{1,0:T(8,128)(2,1)S(1)}, u32[]{:S(2)}, u32[]{:S(2)}) %collective-permute-start.6) | collective-permute-done | bytes 16416 | tf_op jit(solution)/shard_map/ppermute | solution.py:59
  137.4 1.3 collective-permute-start.7
  138.7 6.4 %collective-permute-done.7 = bf16[64,128]{1,0:T(8,128)(2,1)S(1)} collective-permute-done((bf16[64,128]{1,0:T(8,128)(2,1)S(1)}, bf16[64,128]{1,0:T(8,128)(2,1)S(1)}, u32[]{:S(2)}, u32[]{:S(2)}) %collective-permute-start.7) | collective-permute-done | bytes 16416 | tf_op jit(solution)/shard_map/ppermute | solution.py:59
  145.9 1.3 collective-permute-start.8
  147.2 6.5 %collective-permute-done.8 = bf16[64,128]{1,0:T(8,128)(2,1)S(1)} collective-permute-done((bf16[64,128]{1,0:T(8,128)(2,1)S(1)}, bf16[64,128]{1,0:T(8,128)(2,1)S(1)}, u32[]{:S(2)}, u32[]{:S(2)}) %collective-permute-start.8) | collective-permute-done | bytes 16416 | tf_op jit(solution)/shard_map/ppermute | solution.py:59
  153.8 0.8 fusion.22
  154.5 1.3 collective-permute-start.9
  155.8 6.3 %collective-permute-done.9 = bf16[64,128]{1,0:T(8,128)(2,1)S(1)} collective-permute-done((bf16[64,128]{1,0:T(8,128)(2,1)S(1)}, bf16[64,128]{1,0:T(8,128)(2,1)S(1)}, u32[]{:S(2)}, u32[]{:S(2)}) %collective-permute-start.9) | collective-permute-done | bytes 16416 | tf_op jit(solution)/shard_map/ppermute | solution.py:59
  162.9 1.3 collective-permute-start.10
  164.2 6.4 %collective-permute-done.10 = bf16[64,128]{1,0:T(8,128)(2,1)S(1)} collective-permute-done((bf16[64,128]{1,0:T(8,128)(2,1)S(1)}, bf16[64,128]{1,0:T(8,128)(2,1)S(1)}, u32[]{:S(2)}, u32[]{:S(2)}) %collective-permute-start.10) | collective-permute-done | bytes 16416 | tf_op jit(solution)/shard_map/ppermute | solution.py:59
  171.4 1.3 collective-permute-start.11
  172.7 6.4 %collective-permute-done.11 = bf16[64,128]{1,0:T(8,128)(2,1)S(1)} collective-permute-done((bf16[64,128]{1,0:T(8,128)(2,1)S(1)}, bf16[64,128]{1,0:T(8,128)(2,1)S(1)}, u32[]{:S(2)}, u32[]{:S(2)}) %collective-permute-start.11) | collective-permute-done | bytes 16416 | tf_op jit(solution)/shard_map/ppermute | solution.py:59
  179.2 0.8 fusion.19
  179.9 1.3 collective-permute-start.12
  181.2 6.4 %collective-permute-done.12 = bf16[64,128]{1,0:T(8,128)(2,1)S(1)} collective-permute-done((bf16[64,128]{1,0:T(8,128)(2,1)S(1)}, bf16[64,128]{1,0:T(8,128)(2,1)S(1)}, u32[]{:S(2)}, u32[]{:S(2)}) %collective-permute-start.12) | collective-permute-done | bytes 16416 | tf_op jit(solution)/shard_map/ppermute | solution.py:59
  188.4 1.3 collective-permute-start.13
  189.7 6.4 %collective-permute-done.13 = bf16[64,128]{1,0:T(8,128)(2,1)S(1)} collective-permute-done((bf16[64,128]{1,0:T(8,128)(2,1)S(1)}, bf16[64,128]{1,0:T(8,128)(2,1)S(1)}, u32[]{:S(2)}, u32[]{:S(2)}) %collective-permute-start.13) | collective-permute-done | bytes 16416 | tf_op jit(solution)/shard_map/ppermute | solution.py:59
  196.9 1.3 collective-permute-start.14
  198.2 6.4 %collective-permute-done.14 = bf16[64,128]{1,0:T(8,128)(2,1)S(1)} collective-permute-done((bf16[64,128]{1,0:T(8,128)(2,1)S(1)}, bf16[64,128]{1,0:T(8,128)(2,1)S(1)}, u32[]{:S(2)}, u32[]{:S(2)}) %collective-permute-start.14) | collective-permute-done | bytes 16416 | tf_op jit(solution)/shard_map/ppermute | solution.py:59
  204.7 0.8 fusion.16
  205.4 4.3 %collective-permute-start.15 = (bf16[64,128]{1,0:T(8,128)(2,1)S(1)}, bf16[64,128]{1,0:T(8,128)(2,1)S(1)}, u32[]{:S(2)}, u32[]{:S(2)}) collective-permute-start(bf16[64,128]{1,0:T(8,128)(2,1)S(1)} %fusion.16), channel_id=1, source_target_pairs={{240,256},{256,240},{241,257},{257,241},{242,258},{258,242},{243,2... | collective-permute-start | bytes 49160 | tf_op jit(solution)/shard_map/ppermute | solution.py:61
  209.8 1.3 dynamic-slice
  211.7 2.7 collective-permute-done.15
  214.6 23.5 %all-reduce = f32[1024]{0:T(1024)S(1)} all-reduce(f32[1024]{0:T(1024)S(1)} %fusion.100), channel_id=1, replica_groups=mesh['seg'=32,'sec'=16] {'sec'}, use_global_device_ids=true, to_apply=%add | all-reduce | flops 1024 | bytes 8192
  238.2 72.6 %psum.7 = f32[1024]{0:T(1024)} all-reduce(f32[1024]{0:T(1024)S(1)} %all-reduce), channel_id=1, replica_groups=mesh['seg'=32,'sec'=16] {'seg'}, use_global_device_ids=true, to_apply=%region_21.23 | all-reduce | flops 1024 | bytes 8192 | tf_op jit(solution)/shard_map/psum | solution.py:65
  (28 shorter events, 10.8 us)
Async XLA Ops:
  6.5 77.6 %all-gather.6.cloned.1.call-start = ((), (), s32[]{:S(2)}) async-start(), calls=%async_computation | async-start | bytes 2228224 | tf_op jit(solution)/shard_map/all_gather | solution.py:20
  88.0 5.6 %collective-permute-start = (bf16[64,128]{1,0:T(8,128)(2,1)S(1)}, bf16[64,128]{1,0:T(8,128)(2,1)S(1)}, u32[]{:S(2)}, u32[]{:S(2)}) collective-permute-start(bf16[64,128]{1,0:T(8,128)(2,1)S(1)} %fusion.31), channel_id=1, source_target_pairs={{0,16},{16,32},{32,48},{48,64},{64,80},{80,96},{96,112},{112,128},... | collective-permute-start | bytes 49160 | tf_op jit(solution)/shard_map/ppermute | solution.py:59
  94.4 5.6 %collective-permute-start.1 = (bf16[64,128]{1,0:T(8,128)(2,1)S(1)}, bf16[64,128]{1,0:T(8,128)(2,1)S(1)}, u32[]{:S(2)}, u32[]{:S(2)}) collective-permute-start(bf16[64,128]{1,0:T(8,128)(2,1)S(1)} %fusion.30), channel_id=1, source_target_pairs={{0,16},{16,32},{32,48},{48,64},{64,80},{80,96},{96,112},{112,128},... | collective-permute-start | bytes 49160 | tf_op jit(solution)/shard_map/ppermute | solution.py:59
  100.8 5.6 %collective-permute-start.2 = (bf16[64,128]{1,0:T(8,128)(2,1)S(1)}, bf16[64,128]{1,0:T(8,128)(2,1)S(1)}, u32[]{:S(2)}, u32[]{:S(2)}) collective-permute-start(bf16[64,128]{1,0:T(8,128)(2,1)S(1)} %fusion.29), channel_id=1, source_target_pairs={{0,16},{16,32},{32,48},{48,64},{64,80},{80,96},{96,112},{112,128},... | collective-permute-start | bytes 49160 | tf_op jit(solution)/shard_map/ppermute | solution.py:59
  107.2 5.6 %collective-permute-start.3 = (bf16[64,128]{1,0:T(8,128)(2,1)S(1)}, bf16[64,128]{1,0:T(8,128)(2,1)S(1)}, u32[]{:S(2)}, u32[]{:S(2)}) collective-permute-start(bf16[64,128]{1,0:T(8,128)(2,1)S(1)} %fusion.28), channel_id=1, source_target_pairs={{0,16},{16,32},{32,48},{48,64},{64,80},{80,96},{96,112},{112,128},... | collective-permute-start | bytes 49160 | tf_op jit(solution)/shard_map/ppermute | solution.py:59
  113.6 6.1 %collective-permute-start.4 = (bf16[64,128]{1,0:T(8,128)(2,1)S(1)}, bf16[64,128]{1,0:T(8,128)(2,1)S(1)}, u32[]{:S(2)}, u32[]{:S(2)}) collective-permute-start(bf16[64,128]{1,0:T(8,128)(2,1)S(1)} %fusion.27), channel_id=1, source_target_pairs={{0,16},{16,32},{32,48},{48,64},{64,80},{80,96},{96,112},{112,128},... | collective-permute-start | bytes 49160 | tf_op jit(solution)/shard_map/ppermute | solution.py:59
  120.4 7.7 %collective-permute-start.5 = (bf16[64,128]{1,0:T(8,128)(2,1)S(1)}, bf16[64,128]{1,0:T(8,128)(2,1)S(1)}, u32[]{:S(2)}, u32[]{:S(2)}) collective-permute-start(bf16[64,128]{1,0:T(8,128)(2,1)S(1)} %fusion.26), channel_id=1, source_target_pairs={{0,16},{16,32},{32,48},{48,64},{64,80},{80,96},{96,112},{112,128},... | collective-permute-start | bytes 49160 | tf_op jit(solution)/shard_map/ppermute | solution.py:59
  128.9 7.7 %collective-permute-start.6 = (bf16[64,128]{1,0:T(8,128)(2,1)S(1)}, bf16[64,128]{1,0:T(8,128)(2,1)S(1)}, u32[]{:S(2)}, u32[]{:S(2)}) collective-permute-start(bf16[64,128]{1,0:T(8,128)(2,1)S(1)} %fusion.25), channel_id=1, source_target_pairs={{0,16},{16,32},{32,48},{48,64},{64,80},{80,96},{96,112},{112,128},... | collective-permute-start | bytes 49160 | tf_op jit(solution)/shard_map/ppermute | solution.py:59
  137.4 7.7 %collective-permute-start.7 = (bf16[64,128]{1,0:T(8,128)(2,1)S(1)}, bf16[64,128]{1,0:T(8,128)(2,1)S(1)}, u32[]{:S(2)}, u32[]{:S(2)}) collective-permute-start(bf16[64,128]{1,0:T(8,128)(2,1)S(1)} %fusion.24), channel_id=1, source_target_pairs={{0,16},{16,32},{32,48},{48,64},{64,80},{80,96},{96,112},{112,128},... | collective-permute-start | bytes 49160 | tf_op jit(solution)/shard_map/ppermute | solution.py:59
  145.9 7.8 %collective-permute-start.8 = (bf16[64,128]{1,0:T(8,128)(2,1)S(1)}, bf16[64,128]{1,0:T(8,128)(2,1)S(1)}, u32[]{:S(2)}, u32[]{:S(2)}) collective-permute-start(bf16[64,128]{1,0:T(8,128)(2,1)S(1)} %fusion.23), channel_id=1, source_target_pairs={{0,16},{16,32},{32,48},{48,64},{64,80},{80,96},{96,112},{112,128},... | collective-permute-start | bytes 49160 | tf_op jit(solution)/shard_map/ppermute | solution.py:59
  154.5 7.6 %collective-permute-start.9 = (bf16[64,128]{1,0:T(8,128)(2,1)S(1)}, bf16[64,128]{1,0:T(8,128)(2,1)S(1)}, u32[]{:S(2)}, u32[]{:S(2)}) collective-permute-start(bf16[64,128]{1,0:T(8,128)(2,1)S(1)} %fusion.22), channel_id=1, source_target_pairs={{0,16},{16,32},{32,48},{48,64},{64,80},{80,96},{96,112},{112,128},... | collective-permute-start | bytes 49160 | tf_op jit(solution)/shard_map/ppermute | solution.py:59
  162.9 7.7 %collective-permute-start.10 = (bf16[64,128]{1,0:T(8,128)(2,1)S(1)}, bf16[64,128]{1,0:T(8,128)(2,1)S(1)}, u32[]{:S(2)}, u32[]{:S(2)}) collective-permute-start(bf16[64,128]{1,0:T(8,128)(2,1)S(1)} %fusion.21), channel_id=1, source_target_pairs={{0,16},{16,32},{32,48},{48,64},{64,80},{80,96},{96,112},{112,128},... | collective-permute-start | bytes 49160 | tf_op jit(solution)/shard_map/ppermute | solution.py:59
  171.4 7.7 %collective-permute-start.11 = (bf16[64,128]{1,0:T(8,128)(2,1)S(1)}, bf16[64,128]{1,0:T(8,128)(2,1)S(1)}, u32[]{:S(2)}, u32[]{:S(2)}) collective-permute-start(bf16[64,128]{1,0:T(8,128)(2,1)S(1)} %fusion.20), channel_id=1, source_target_pairs={{0,16},{16,32},{32,48},{48,64},{64,80},{80,96},{96,112},{112,128},... | collective-permute-start | bytes 49160 | tf_op jit(solution)/shard_map/ppermute | solution.py:59
  179.9 7.7 %collective-permute-start.12 = (bf16[64,128]{1,0:T(8,128)(2,1)S(1)}, bf16[64,128]{1,0:T(8,128)(2,1)S(1)}, u32[]{:S(2)}, u32[]{:S(2)}) collective-permute-start(bf16[64,128]{1,0:T(8,128)(2,1)S(1)} %fusion.19), channel_id=1, source_target_pairs={{0,16},{16,32},{32,48},{48,64},{64,80},{80,96},{96,112},{112,128},... | collective-permute-start | bytes 49160 | tf_op jit(solution)/shard_map/ppermute | solution.py:59
  188.4 7.7 %collective-permute-start.13 = (bf16[64,128]{1,0:T(8,128)(2,1)S(1)}, bf16[64,128]{1,0:T(8,128)(2,1)S(1)}, u32[]{:S(2)}, u32[]{:S(2)}) collective-permute-start(bf16[64,128]{1,0:T(8,128)(2,1)S(1)} %fusion.18), channel_id=1, source_target_pairs={{0,16},{16,32},{32,48},{48,64},{64,80},{80,96},{96,112},{112,128},... | collective-permute-start | bytes 49160 | tf_op jit(solution)/shard_map/ppermute | solution.py:59
  196.9 7.7 %collective-permute-start.14 = (bf16[64,128]{1,0:T(8,128)(2,1)S(1)}, bf16[64,128]{1,0:T(8,128)(2,1)S(1)}, u32[]{:S(2)}, u32[]{:S(2)}) collective-permute-start(bf16[64,128]{1,0:T(8,128)(2,1)S(1)} %fusion.17), channel_id=1, source_target_pairs={{0,16},{16,32},{32,48},{48,64},{64,80},{80,96},{96,112},{112,128},... | collective-permute-start | bytes 49160 | tf_op jit(solution)/shard_map/ppermute | solution.py:59
  205.4 9.0 %collective-permute-start.15 = (bf16[64,128]{1,0:T(8,128)(2,1)S(1)}, bf16[64,128]{1,0:T(8,128)(2,1)S(1)}, u32[]{:S(2)}, u32[]{:S(2)}) collective-permute-start(bf16[64,128]{1,0:T(8,128)(2,1)S(1)} %fusion.16), channel_id=1, source_target_pairs={{240,256},{256,240},{241,257},{257,241},{242,258},{258,242},{243,2... | collective-permute-start | bytes 49160 | tf_op jit(solution)/shard_map/ppermute | solution.py:61
Sparse Core Ops, SparseCore 0:
  9.5 47.2 all-gather.5
where the time goes:
time: 320 us; the launch traced here: 318 us
  blocking collectives  168 us (52%)
  waiting for transfers between devices  89.3 us (28%)
  starting transfers between devices  23.7 us (7%)
  between operations  14.4 us (4%)
  matrix products  12.1 us (4%)
  local copies, waits for them, and re-layouts  7.99 us (2%)
    ppermute x15, waiting for transfers between devices, per_device(): vector = lax.ppermute(vector, 'seg', chain)  86.5 us
    psum x1, blocking collectives, per_device(): return lax.psum(gathered, 'seg')  72.6 us
    all_gather x1, blocking collectives, per_device(): occ_group = lax.all_gather(occ_mine, 'seg', axis=1, tiled=True)  34.2 us
    unnamed x1, blocking collectives  23.5 us
    all_gather x1, blocking collectives, per_device(): rights = lax.all_gather(right_edge, 'sec', axis=0, tiled=True)  23.3 us
    ppermute x15, starting transfers between devices, per_device(): vector = lax.ppermute(vector, 'seg', chain)  19.4 us
    all_gather x1, blocking collectives, per_device(): lefts = lax.all_gather(left_edge, 'sec', axis=0, tiled=True)  14.6 us
    dot_general x16, matrix products, apply(): jnp.einsum('kqa,nqab->knb', spread, oriented, preferred_element_type=jnp....  12.1 us
  transfers between devices with their start and end apart: 17, of which 16 were waited for; matrix products, arithmetic and copies ran while one was open for 2% of the time, Pallas kernels for 0%

commit v1 on v0

--- a/solution.py
+++ b/solution.py
@@ -62,7 +62,7 @@
     amp = jnp.sum(vector.astype(jnp.float32) * other.astype(jnp.float32), axis=1)
     amp = jnp.where(seg_index == half_count - 1, amp, jnp.zeros_like(amp))
     gathered = lax.all_gather(amp, "sec", axis=0, tiled=True)
-    return lax.psum(gathered, "seg")
+    return jnp.sum(lax.all_gather(gathered, "seg"), axis=0)
 
 
 def solution(mesh):

time: 320 us -> 289 us (0.903)
  the two profiles are of different devices: /device:TPU:32 before, /device:TPU:24 now
where the time goes in v1:
time: 289 us; the launch traced here: 287 us
  blocking collectives  134 us (46%)
  waiting for transfers between devices  87.1 us (30%)
  starting transfers between devices  29.7 us (10%)
  between operations  14.4 us (5%)
  matrix products  12.1 us (4%)
  local copies, waits for them, and re-layouts  6.56 us (2%)
    ppermute x15, waiting for transfers between devices, per_device(): vector = lax.ppermute(vector, 'seg', chain)  87.1 us
    all_gather x1, blocking collectives, per_device(): return jnp.sum(lax.all_gather(gathered, 'seg'), axis=0)  37.2 us
    all_gather x1, blocking collectives, per_device(): occ_group = lax.all_gather(occ_mine, 'seg', axis=1, tiled=True)  35.6 us
    ppermute x15, starting transfers between devices, per_device(): vector = lax.ppermute(vector, 'seg', chain)  29.1 us
    unnamed x1, blocking collectives  23.5 us
    all_gather x1, blocking collectives, per_device(): rights = lax.all_gather(right_edge, 'sec', axis=0, tiled=True)  23.3 us
    all_gather x1, blocking collectives, per_device(): lefts = lax.all_gather(left_edge, 'sec', axis=0, tiled=True)  14.6 us
    dot_general x16, matrix products, apply(): jnp.einsum('kqa,nqab->knb', spread, oriented, preferred_element_type=jnp....  12.1 us
  transfers between devices with their start and end apart: 17, of which 15 were waited for; matrix products, arithmetic and copies ran while one was open for 2% of the time, Pallas kernels for 0%

profile of v1, /device:TPU:24, one launch (start us, length us, event | category | flops | bytes accessed | tf_op | source)
XLA Modules:
  0.0 286.8 jit_solution(366118645245599922)
XLA Ops:
  6.5 1.7 copy.33
  8.2 23.3 %all-gather.3 = bf16[16,1,128]{2,1,0:T(2,128)(2,1)S(1)} all-gather(bf16[1,1,128]{2,1,0:T(2,128)(2,1)} %bitcast.200), channel_id=1, replica_groups=mesh['seg'=32,'sec'=16] {'sec'}, dimensions={0}, use_global_device_ids=true | all-gather | bytes 4352 | tf_op jit(solution)/shard_map/all_gather | solution.py:23
  31.6 14.6 %all-gather.2 = bf16[16,1,128]{2,1,0:T(2,128)(2,1)S(1)} all-gather(bf16[1,1,128]{2,1,0:T(2,128)(2,1)} %bitcast.201), channel_id=1, replica_groups=mesh['seg'=32,'sec'=16] {'sec'}, dimensions={0}, use_global_device_ids=true | all-gather | bytes 4352 | tf_op jit(solution)/shard_map/all_gather | solution.py:22
  46.9 35.6 %all-gather.4 = s32[32,1,64]{2,1,0:T(1,128)S(1)} all-gather(s32[1,1,64]{2,1,0:T(1,128)S(1)} %get-tuple-element.18), channel_id=1, replica_groups=mesh['seg'=32,'sec'=16] {'seg'}, dimensions={0}, use_global_device_ids=true | all-gather | bytes 8448 | tf_op jit(solution)/shard_map/all_gather | solution.py:26
  82.7 0.8 compare_and_fusion.1
  84.7 0.8 and_select_fusion
  85.6 1.6 conditional.1
  85.6 1.6 copy.90
  88.0 2.2 collective-permute-start
  90.2 5.5 %collective-permute-done = bf16[64,128]{1,0:T(8,128)(2,1)S(1)} collective-permute-done((bf16[64,128]{1,0:T(8,128)(2,1)S(1)}, bf16[64,128]{1,0:T(8,128)(2,1)S(1)}, u32[]{:S(2)}, u32[]{:S(2)}) %collective-permute-start) | collective-permute-done | bytes 16416 | tf_op jit(solution)/shard_map/ppermute | solution.py:59
  95.7 0.8 fusion.30
  96.5 1.9 collective-permute-start.1
  98.4 5.8 %collective-permute-done.1 = bf16[64,128]{1,0:T(8,128)(2,1)S(1)} collective-permute-done((bf16[64,128]{1,0:T(8,128)(2,1)S(1)}, bf16[64,128]{1,0:T(8,128)(2,1)S(1)}, u32[]{:S(2)}, u32[]{:S(2)}) %collective-permute-start.1) | collective-permute-done | bytes 16416 | tf_op jit(solution)/shard_map/ppermute | solution.py:59
  105.0 1.9 collective-permute-start.2
  106.9 5.8 %collective-permute-done.2 = bf16[64,128]{1,0:T(8,128)(2,1)S(1)} collective-permute-done((bf16[64,128]{1,0:T(8,128)(2,1)S(1)}, bf16[64,128]{1,0:T(8,128)(2,1)S(1)}, u32[]{:S(2)}, u32[]{:S(2)}) %collective-permute-start.2) | collective-permute-done | bytes 16416 | tf_op jit(solution)/shard_map/ppermute | solution.py:59
  113.5 1.9 collective-permute-start.3
  115.4 5.8 %collective-permute-done.3 = bf16[64,128]{1,0:T(8,128)(2,1)S(1)} collective-permute-done((bf16[64,128]{1,0:T(8,128)(2,1)S(1)}, bf16[64,128]{1,0:T(8,128)(2,1)S(1)}, u32[]{:S(2)}, u32[]{:S(2)}) %collective-permute-start.3) | collective-permute-done | bytes 16416 | tf_op jit(solution)/shard_map/ppermute | solution.py:59
  122.0 1.9 collective-permute-start.4
  123.9 5.8 %collective-permute-done.4 = bf16[64,128]{1,0:T(8,128)(2,1)S(1)} collective-permute-done((bf16[64,128]{1,0:T(8,128)(2,1)S(1)}, bf16[64,128]{1,0:T(8,128)(2,1)S(1)}, u32[]{:S(2)}, u32[]{:S(2)}) %collective-permute-start.4) | collective-permute-done | bytes 16416 | tf_op jit(solution)/shard_map/ppermute | solution.py:59
  129.7 0.8 fusion.26
  130.5 1.9 collective-permute-start.5
  132.4 5.8 %collective-permute-done.5 = bf16[64,128]{1,0:T(8,128)(2,1)S(1)} collective-permute-done((bf16[64,128]{1,0:T(8,128)(2,1)S(1)}, bf16[64,128]{1,0:T(8,128)(2,1)S(1)}, u32[]{:S(2)}, u32[]{:S(2)}) %collective-permute-start.5) | collective-permute-done | bytes 16416 | tf_op jit(solution)/shard_map/ppermute | solution.py:59
  138.2 0.8 fusion.25
  139.0 1.9 collective-permute-start.6
  140.9 5.9 %collective-permute-done.6 = bf16[64,128]{1,0:T(8,128)(2,1)S(1)} collective-permute-done((bf16[64,128]{1,0:T(8,128)(2,1)S(1)}, bf16[64,128]{1,0:T(8,128)(2,1)S(1)}, u32[]{:S(2)}, u32[]{:S(2)}) %collective-permute-start.6) | collective-permute-done | bytes 16416 | tf_op jit(solution)/shard_map/ppermute | solution.py:59
  147.6 1.9 collective-permute-start.7
  149.6 5.8 %collective-permute-done.7 = bf16[64,128]{1,0:T(8,128)(2,1)S(1)} collective-permute-done((bf16[64,128]{1,0:T(8,128)(2,1)S(1)}, bf16[64,128]{1,0:T(8,128)(2,1)S(1)}, u32[]{:S(2)}, u32[]{:S(2)}) %collective-permute-start.7) | collective-permute-done | bytes 16416 | tf_op jit(solution)/shard_map/ppermute | solution.py:59
  155.4 0.8 fusion.23
  156.1 1.9 collective-permute-start.8
  158.1 5.8 %collective-permute-done.8 = bf16[64,128]{1,0:T(8,128)(2,1)S(1)} collective-permute-done((bf16[64,128]{1,0:T(8,128)(2,1)S(1)}, bf16[64,128]{1,0:T(8,128)(2,1)S(1)}, u32[]{:S(2)}, u32[]{:S(2)}) %collective-permute-start.8) | collective-permute-done | bytes 16416 | tf_op jit(solution)/shard_map/ppermute | solution.py:59
  163.9 0.8 fusion.22
  164.6 1.9 collective-permute-start.9
  166.6 5.8 %collective-permute-done.9 = bf16[64,128]{1,0:T(8,128)(2,1)S(1)} collective-permute-done((bf16[64,128]{1,0:T(8,128)(2,1)S(1)}, bf16[64,128]{1,0:T(8,128)(2,1)S(1)}, u32[]{:S(2)}, u32[]{:S(2)}) %collective-permute-start.9) | collective-permute-done | bytes 16416 | tf_op jit(solution)/shard_map/ppermute | solution.py:59
  173.1 1.9 collective-permute-start.10
  175.1 5.8 %collective-permute-done.10 = bf16[64,128]{1,0:T(8,128)(2,1)S(1)} collective-permute-done((bf16[64,128]{1,0:T(8,128)(2,1)S(1)}, bf16[64,128]{1,0:T(8,128)(2,1)S(1)}, u32[]{:S(2)}, u32[]{:S(2)}) %collective-permute-start.10) | collective-permute-done | bytes 16416 | tf_op jit(solution)/shard_map/ppermute | solution.py:59
  180.9 0.8 fusion.20
  181.6 1.9 collective-permute-start.11
  183.6 5.8 %collective-permute-done.11 = bf16[64,128]{1,0:T(8,128)(2,1)S(1)} collective-permute-done((bf16[64,128]{1,0:T(8,128)(2,1)S(1)}, bf16[64,128]{1,0:T(8,128)(2,1)S(1)}, u32[]{:S(2)}, u32[]{:S(2)}) %collective-permute-start.11) | collective-permute-done | bytes 16416 | tf_op jit(solution)/shard_map/ppermute | solution.py:59
  189.4 0.8 fusion.19
  190.1 1.9 collective-permute-start.12
  192.1 5.8 %collective-permute-done.12 = bf16[64,128]{1,0:T(8,128)(2,1)S(1)} collective-permute-done((bf16[64,128]{1,0:T(8,128)(2,1)S(1)}, bf16[64,128]{1,0:T(8,128)(2,1)S(1)}, u32[]{:S(2)}, u32[]{:S(2)}) %collective-permute-start.12) | collective-permute-done | bytes 16416 | tf_op jit(solution)/shard_map/ppermute | solution.py:59
  198.7 1.9 collective-permute-start.13
  200.6 5.8 %collective-permute-done.13 = bf16[64,128]{1,0:T(8,128)(2,1)S(1)} collective-permute-done((bf16[64,128]{1,0:T(8,128)(2,1)S(1)}, bf16[64,128]{1,0:T(8,128)(2,1)S(1)}, u32[]{:S(2)}, u32[]{:S(2)}) %collective-permute-start.13) | collective-permute-done | bytes 16416 | tf_op jit(solution)/shard_map/ppermute | solution.py:59
  207.2 1.9 collective-permute-start.14
  209.1 5.8 %collective-permute-done.14 = bf16[64,128]{1,0:T(8,128)(2,1)S(1)} collective-permute-done((bf16[64,128]{1,0:T(8,128)(2,1)S(1)}, bf16[64,128]{1,0:T(8,128)(2,1)S(1)}, u32[]{:S(2)}, u32[]{:S(2)}) %collective-permute-start.14) | collective-permute-done | bytes 16416 | tf_op jit(solution)/shard_map/ppermute | solution.py:59
  216.3 1.3 dynamic-slice
  218.5 23.5 %all-reduce = f32[1024]{0:T(1024)S(1)} all-reduce(f32[1024]{0:T(1024)S(1)} %fusion.100), channel_id=1, replica_groups=mesh['seg'=32,'sec'=16] {'sec'}, use_global_device_ids=true, to_apply=%add | all-reduce | flops 1024 | bytes 8192
  242.0 37.2 %all-gather.1 = f32[32768]{0:T(1024)S(1)} all-gather(f32[1024]{0:T(1024)S(1)} %all-reduce), channel_id=3, replica_groups=mesh['seg'=32,'sec'=16] {'seg'}, dimensions={0}, use_global_device_ids=true | all-gather | bytes 135168 | tf_op jit(solution)/shard_map/all_gather | solution.py:65
  (30 shorter events, 10.5 us)
Async XLA Ops:
  6.5 79.1 %all-gather.7.cloned.1.call-start = ((), (), s32[]{:S(2)}) async-start(), calls=%async_computation | async-start | bytes 2228224 | tf_op jit(solution)/shard_map/all_gather | solution.py:20
  88.0 7.7 %collective-permute-start = (bf16[64,128]{1,0:T(8,128)(2,1)S(1)}, bf16[64,128]{1,0:T(8,128)(2,1)S(1)}, u32[]{:S(2)}, u32[]{:S(2)}) collective-permute-start(bf16[64,128]{1,0:T(8,128)(2,1)S(1)} %fusion.31), channel_id=1, source_target_pairs={{0,16},{16,32},{32,48},{48,64},{64,80},{80,96},{96,112},{112,128},... | collective-permute-start | bytes 49160 | tf_op jit(solution)/shard_map/ppermute | solution.py:59
  96.5 7.7 %collective-permute-start.1 = (bf16[64,128]{1,0:T(8,128)(2,1)S(1)}, bf16[64,128]{1,0:T(8,128)(2,1)S(1)}, u32[]{:S(2)}, u32[]{:S(2)}) collective-permute-start(bf16[64,128]{1,0:T(8,128)(2,1)S(1)} %fusion.30), channel_id=1, source_target_pairs={{0,16},{16,32},{32,48},{48,64},{64,80},{80,96},{96,112},{112,128},... | collective-permute-start | bytes 49160 | tf_op jit(solution)/shard_map/ppermute | solution.py:59
  105.0 7.7 %collective-permute-start.2 = (bf16[64,128]{1,0:T(8,128)(2,1)S(1)}, bf16[64,128]{1,0:T(8,128)(2,1)S(1)}, u32[]{:S(2)}, u32[]{:S(2)}) collective-permute-start(bf16[64,128]{1,0:T(8,128)(2,1)S(1)} %fusion.29), channel_id=1, source_target_pairs={{0,16},{16,32},{32,48},{48,64},{64,80},{80,96},{96,112},{112,128},... | collective-permute-start | bytes 49160 | tf_op jit(solution)/shard_map/ppermute | solution.py:59
  113.5 7.7 %collective-permute-start.3 = (bf16[64,128]{1,0:T(8,128)(2,1)S(1)}, bf16[64,128]{1,0:T(8,128)(2,1)S(1)}, u32[]{:S(2)}, u32[]{:S(2)}) collective-permute-start(bf16[64,128]{1,0:T(8,128)(2,1)S(1)} %fusion.28), channel_id=1, source_target_pairs={{0,16},{16,32},{32,48},{48,64},{64,80},{80,96},{96,112},{112,128},... | collective-permute-start | bytes 49160 | tf_op jit(solution)/shard_map/ppermute | solution.py:59
  122.0 7.7 %collective-permute-start.4 = (bf16[64,128]{1,0:T(8,128)(2,1)S(1)}, bf16[64,128]{1,0:T(8,128)(2,1)S(1)}, u32[]{:S(2)}, u32[]{:S(2)}) collective-permute-start(bf16[64,128]{1,0:T(8,128)(2,1)S(1)} %fusion.27), channel_id=1, source_target_pairs={{0,16},{16,32},{32,48},{48,64},{64,80},{80,96},{96,112},{112,128},... | collective-permute-start | bytes 49160 | tf_op jit(solution)/shard_map/ppermute | solution.py:59
  130.5 7.7 %collective-permute-start.5 = (bf16[64,128]{1,0:T(8,128)(2,1)S(1)}, bf16[64,128]{1,0:T(8,128)(2,1)S(1)}, u32[]{:S(2)}, u32[]{:S(2)}) collective-permute-start(bf16[64,128]{1,0:T(8,128)(2,1)S(1)} %fusion.26), channel_id=1, source_target_pairs={{0,16},{16,32},{32,48},{48,64},{64,80},{80,96},{96,112},{112,128},... | collective-permute-start | bytes 49160 | tf_op jit(solution)/shard_map/ppermute | solution.py:59
  139.0 7.9 %collective-permute-start.6 = (bf16[64,128]{1,0:T(8,128)(2,1)S(1)}, bf16[64,128]{1,0:T(8,128)(2,1)S(1)}, u32[]{:S(2)}, u32[]{:S(2)}) collective-permute-start(bf16[64,128]{1,0:T(8,128)(2,1)S(1)} %fusion.25), channel_id=1, source_target_pairs={{0,16},{16,32},{32,48},{48,64},{64,80},{80,96},{96,112},{112,128},... | collective-permute-start | bytes 49160 | tf_op jit(solution)/shard_map/ppermute | solution.py:59
  147.6 7.7 %collective-permute-start.7 = (bf16[64,128]{1,0:T(8,128)(2,1)S(1)}, bf16[64,128]{1,0:T(8,128)(2,1)S(1)}, u32[]{:S(2)}, u32[]{:S(2)}) collective-permute-start(bf16[64,128]{1,0:T(8,128)(2,1)S(1)} %fusion.24), channel_id=1, source_target_pairs={{0,16},{16,32},{32,48},{48,64},{64,80},{80,96},{96,112},{112,128},... | collective-permute-start | bytes 49160 | tf_op jit(solution)/shard_map/ppermute | solution.py:59
  156.1 7.7 %collective-permute-start.8 = (bf16[64,128]{1,0:T(8,128)(2,1)S(1)}, bf16[64,128]{1,0:T(8,128)(2,1)S(1)}, u32[]{:S(2)}, u32[]{:S(2)}) collective-permute-start(bf16[64,128]{1,0:T(8,128)(2,1)S(1)} %fusion.23), channel_id=1, source_target_pairs={{0,16},{16,32},{32,48},{48,64},{64,80},{80,96},{96,112},{112,128},... | collective-permute-start | bytes 49160 | tf_op jit(solution)/shard_map/ppermute | solution.py:59
  164.6 7.7 %collective-permute-start.9 = (bf16[64,128]{1,0:T(8,128)(2,1)S(1)}, bf16[64,128]{1,0:T(8,128)(2,1)S(1)}, u32[]{:S(2)}, u32[]{:S(2)}) collective-permute-start(bf16[64,128]{1,0:T(8,128)(2,1)S(1)} %fusion.22), channel_id=1, source_target_pairs={{0,16},{16,32},{32,48},{48,64},{64,80},{80,96},{96,112},{112,128},... | collective-permute-start | bytes 49160 | tf_op jit(solution)/shard_map/ppermute | solution.py:59
  173.1 7.7 %collective-permute-start.10 = (bf16[64,128]{1,0:T(8,128)(2,1)S(1)}, bf16[64,128]{1,0:T(8,128)(2,1)S(1)}, u32[]{:S(2)}, u32[]{:S(2)}) collective-permute-start(bf16[64,128]{1,0:T(8,128)(2,1)S(1)} %fusion.21), channel_id=1, source_target_pairs={{0,16},{16,32},{32,48},{48,64},{64,80},{80,96},{96,112},{112,128},... | collective-permute-start | bytes 49160 | tf_op jit(solution)/shard_map/ppermute | solution.py:59
  181.6 7.7 %collective-permute-start.11 = (bf16[64,128]{1,0:T(8,128)(2,1)S(1)}, bf16[64,128]{1,0:T(8,128)(2,1)S(1)}, u32[]{:S(2)}, u32[]{:S(2)}) collective-permute-start(bf16[64,128]{1,0:T(8,128)(2,1)S(1)} %fusion.20), channel_id=1, source_target_pairs={{0,16},{16,32},{32,48},{48,64},{64,80},{80,96},{96,112},{112,128},... | collective-permute-start | bytes 49160 | tf_op jit(solution)/shard_map/ppermute | solution.py:59
  190.1 7.7 %collective-permute-start.12 = (bf16[64,128]{1,0:T(8,128)(2,1)S(1)}, bf16[64,128]{1,0:T(8,128)(2,1)S(1)}, u32[]{:S(2)}, u32[]{:S(2)}) collective-permute-start(bf16[64,128]{1,0:T(8,128)(2,1)S(1)} %fusion.19), channel_id=1, source_target_pairs={{0,16},{16,32},{32,48},{48,64},{64,80},{80,96},{96,112},{112,128},... | collective-permute-start | bytes 49160 | tf_op jit(solution)/shard_map/ppermute | solution.py:59
  198.7 7.7 %collective-permute-start.13 = (bf16[64,128]{1,0:T(8,128)(2,1)S(1)}, bf16[64,128]{1,0:T(8,128)(2,1)S(1)}, u32[]{:S(2)}, u32[]{:S(2)}) collective-permute-start(bf16[64,128]{1,0:T(8,128)(2,1)S(1)} %fusion.18), channel_id=1, source_target_pairs={{0,16},{16,32},{32,48},{48,64},{64,80},{80,96},{96,112},{112,128},... | collective-permute-start | bytes 49160 | tf_op jit(solution)/shard_map/ppermute | solution.py:59
  207.2 7.7 %collective-permute-start.14 = (bf16[64,128]{1,0:T(8,128)(2,1)S(1)}, bf16[64,128]{1,0:T(8,128)(2,1)S(1)}, u32[]{:S(2)}, u32[]{:S(2)}) collective-permute-start(bf16[64,128]{1,0:T(8,128)(2,1)S(1)} %fusion.17), channel_id=1, source_target_pairs={{0,16},{16,32},{32,48},{48,64},{64,80},{80,96},{96,112},{112,128},... | collective-permute-start | bytes 49160 | tf_op jit(solution)/shard_map/ppermute | solution.py:59
  215.7 2.6 collective-permute-start.15
Sparse Core Ops, SparseCore 0:
  9.5 47.2 all-gather.6
